TPU v7x, 32 devices: a whole 2x2x4 slice. The times are simulated.
32 devices in a mesh: groups: 2 (over x), date: 8 (over z, y), row: 2 (over core).
Axes of the slice: x: 2, y: 2, z: 4, core: 2. Of those that a mesh axis runs over, the one named last changes fastest.
Arguments:
- scenes: bfloat16 [16, 4, 512, 1024], P(('groups', 'date'), None, 'row'), parts along dimension 0, may hold values from -6 to 6
- resample_taps: float32 [2, 4, 7], replicated, may hold values from 0 to 0.35
- clear_mask: int32 [16, 128, 8], P('groups', ('row', 'date')), parts along dimension 0, may hold values 0 or 1
Outputs:
- smooth_fine: bfloat16 [16, 4, 512, 1024], P('groups', None, ('row', 'date')), parts along dimension 0
- smooth_half: bfloat16 [16, 4, 256, 512], P('groups', None, ('row', 'date')), parts along dimension 0
- smooth_quarter: bfloat16 [16, 4, 128, 256], P('groups', None, ('row', 'date')), parts along dimension 0
There are 2 independent parts, one for each index of `groups`. A program takes and returns all parts, laid end to end along the dimension named above; an argument that names none is the same for every part. Nothing has to cross between parts.
Inputs may be any that keep to these rules, and one draw needn't show every extreme that they name: `clear_mask`: 1 marks a clear block, 0 a cloudy one.
All inputs are finite; a program needn't handle non-finite values.
Results may differ from a plain program's by a relative error of at most 0.005.
Values may be sent and summed in bfloat16 or wider, within the bound.
No kernel may reach another device: no remote copies, remote signals or barrier semaphores. Data moves between devices by JAX's collectives and lax.ppermute only.
A program may use at most 128 MiB of HBM per device.

v0:
```python
import math
import jax
import jax.numpy as jnp
from jax import lax
from jax.sharding import PartitionSpec as P

gap_weights = [math.exp(-((k - 4) ** 2) / 8.0) for k in range(9)]
savgol_coeffs = [c / 231.0 for c in [-21.0, 14.0, 39.0, 54.0, 59.0, 54.0, 39.0, 14.0, -21.0]]
pyramid_filter = [0.125, 0.375, 0.375, 0.125]


def padded(block, sides, width):
    for axis, dim in sides:
        count = lax.axis_size(axis)
        forward = [(i, i + 1) for i in range(count - 1)]
        backward = [(target, source) for source, target in forward]
        low = lax.ppermute(
            lax.slice_in_dim(block, block.shape[dim] - width, None, axis=dim), axis, forward
        )
        high = lax.ppermute(lax.slice_in_dim(block, 0, width, axis=dim), axis, backward)
        block = jnp.concatenate([low, block, high], axis=dim)
    return block


def valid_taps(values, taps, axis):
    count = values.shape[axis] - 6
    total = jnp.zeros(values.shape[:axis] + (count,) + values.shape[axis + 1 :], jnp.float32)
    for k in range(7):
        shape = [1] * values.ndim
        shape[-3] = taps.shape[0]
        total = total + taps[:, k].reshape(shape) * lax.slice_in_dim(values, k, k + count, 1, axis)
    return total


def column_resample(values, taps):
    width = values.shape[3]
    source = lax.broadcasted_iota(jnp.int32, (width, width), 0)
    target = lax.broadcasted_iota(jnp.int32, (width, width), 1)
    offset = source - target + 3
    table = jnp.zeros((taps.shape[0], width, width), jnp.float32)
    for k in range(7):
        table = table + taps[:, k][:, None, None] * (offset == k).astype(jnp.float32)[None]
    return jnp.einsum(
        "tbrc,bcd->tbrd", values.astype(jnp.float32), table, precision=lax.Precision.HIGHEST
    )


def halve_columns(values):
    width = values.shape[3]
    source = lax.broadcasted_iota(jnp.int32, (width, width // 2), 0)
    target = lax.broadcasted_iota(jnp.int32, (width, width // 2), 1)
    place = source - 2 * target + 1
    table = jnp.zeros((width, width // 2), jnp.float32)
    for p in range(4):
        table = table + pyramid_filter[p] * (place == p).astype(jnp.float32)
    return jnp.dot(values, table, precision=lax.Precision.HIGHEST)


def halve_rows(extended):
    pairs_count = extended.shape[2] // 2
    pairs = extended.reshape(extended.shape[:2] + (pairs_count, 2) + extended.shape[3:])
    even = pairs[:, :, :, 0]
    odd = pairs[:, :, :, 1]
    return (
        pyramid_filter[0] * even[:, :, :-1]
        + pyramid_filter[1] * odd[:, :, :-1]
        + pyramid_filter[2] * even[:, :, 1:]
        + pyramid_filter[3] * odd[:, :, 1:]
    )


def decimate_rim(extended):
    return halve_columns(halve_rows(extended))


def keep_rows(values, first, total):
    places = first + lax.iota(jnp.int32, values.shape[2])
    inside = (places >= 0) & (places < total)
    return jnp.where(inside[None, None, :, None], values, 0.0)


def smooth(level, clear):
    values = level.astype(jnp.float32)
    dates = values.shape[0]
    clear4 = clear[:, None]
    weight = 0.1 + 0.9 * clear4
    weighted = jnp.pad(weight * values, ((4, 4), (0, 0), (0, 0), (0, 0)))
    weight_pad = jnp.pad(weight, ((4, 4), (0, 0), (0, 0), (0, 0)))
    numer = jnp.zeros_like(values)
    denom = jnp.zeros_like(weight)
    for k in range(9):
        numer = numer + gap_weights[k] * weighted[k : k + dates]
        denom = denom + gap_weights[k] * weight_pad[k : k + dates]
    filled = clear4 * values + (1.0 - clear4) * (numer / denom)
    edged = jnp.pad(filled, ((4, 4), (0, 0), (0, 0), (0, 0)), mode="edge")
    result = jnp.zeros_like(values)
    for k in range(9):
        result = result + savgol_coeffs[k] * edged[k : k + dates]
    return result.astype(jnp.bfloat16)


def expand_mask(clear_mask, row_rep, col_rep):
    grown = jnp.repeat(jnp.repeat(clear_mask, row_rep, axis=1), col_rep, axis=2)
    return grown.astype(jnp.float32)


def local(scenes, resample_taps, clear_mask):
    rows = scenes.shape[2]
    extended = padded(scenes, (("row", 2),), 6)
    across = column_resample(extended, resample_taps[0])
    resampled_wide = valid_taps(across, resample_taps[1], 2)
    band_index = lax.axis_index("row")
    total_rows = rows * lax.axis_size("row")
    resampled_wide = keep_rows(resampled_wide, band_index * rows - 3, total_rows)
    half_wide = decimate_rim(resampled_wide)
    half_wide = keep_rows(half_wide, band_index * (rows // 2) - 1, total_rows // 2)
    resampled = resampled_wide[:, :, 3 : 3 + rows]
    half = half_wide[:, :, 1 : 1 + rows // 2]
    quarter = decimate_rim(half_wide)
    level_zero = resampled.astype(jnp.bfloat16)
    level_one = half.astype(jnp.bfloat16)
    level_two = quarter.astype(jnp.bfloat16)
    clear_fine = expand_mask(clear_mask, 4, 128)
    clear_half = expand_mask(clear_mask, 2, 64)
    clear_quarter = expand_mask(clear_mask, 1, 32)
    smooth_fine = smooth(
        lax.all_to_all(level_zero, "date", split_axis=2, concat_axis=0, tiled=True), clear_fine
    )
    smooth_half = smooth(
        lax.all_to_all(level_one, "date", split_axis=2, concat_axis=0, tiled=True), clear_half
    )
    smooth_quarter = smooth(
        lax.all_to_all(level_two, "date", split_axis=2, concat_axis=0, tiled=True), clear_quarter
    )
    return (smooth_fine, smooth_half, smooth_quarter)


def solution(mesh):
    in_specs = (P(("groups", "date"), None, "row", None), P(), P("groups", ("row", "date"), None))
    out_specs = (
        P("groups", None, ("row", "date"), None),
        P("groups", None, ("row", "date"), None),
        P("groups", None, ("row", "date"), None),
    )
    return jax.shard_map(local, mesh=mesh, in_specs=in_specs, out_specs=out_specs, check_vma=False)
```

profile of v0, /device:TPU:0, one launch (start us, length us, event | category | flops | bytes accessed | tf_op | source)
XLA Modules:
  0.0 176.9 jit_solution(12469758215546184341)
XLA Ops:
  1.5 2.4 %collective-permute-start = (bf16[1,4,6,1024]{3,2,1,0:T(8,128)(2,1)S(1)}, bf16[1,4,6,1024]{3,2,1,0:T(8,128)(2,1)S(1)}, u32[]{:S(2)}, u32[]{:S(2)}) collective-permute-start(bf16[1,4,6,1024]{3,2,1,0:T(8,128)(2,1)S(1)} %get-tuple-element.21), channel_id=1, source_target_pairs={{0,1},{2,3},{4,5},{6,7},{8,9},{10,11},{12,13},{14,15},{16,17},{18,... | collective-permute-start | bytes 147464 | tf_op jit(solution)/shard_map/ppermute | solution.py:17
  5.2 4.3 %fusion.83 = (f32[1024,1024]{1,0:T(8,128)}, f32[1024,1024]{1,0:T(8,128)}) fusion(), kind=kLoop, calls=%fused_computation.132 | loop fusion | flops 6291456 | bytes 8388608 | tf_op jit(solution)/shard_map/convert_element_type | solution.py:42
  9.5 4.3 %fusion.85 = (f32[1024,1024]{1,0:T(8,128)}, f32[1024,1024]{1,0:T(8,128)}) fusion(), kind=kLoop, calls=%fused_computation.134 | loop fusion | flops 6291456 | bytes 8388608 | tf_op jit(solution)/shard_map/convert_element_type | solution.py:42
  13.8 4.3 %fusion.87 = (f32[1024,1024]{1,0:T(8,128)}, f32[1024,1024]{1,0:T(8,128)}) fusion(), kind=kLoop, calls=%fused_computation.136 | loop fusion | flops 6291456 | bytes 8388608 | tf_op jit(solution)/shard_map/convert_element_type | solution.py:42
  18.2 2.5 %fusion.89 = f32[1024,1024]{1,0:T(8,128)} fusion(), kind=kLoop, calls=%fused_computation.138 | loop fusion | flops 4194304 | bytes 4194304 | tf_op jit(solution)/shard_map/convert_element_type | solution.py:42
  21.1 23.9 %fusion.96 = f32[1,4,268,1024]{3,2,1,0:T(8,128)S(1)} fusion(bf16[1,4,6,1024]{3,2,1,0:T(8,128)(2,1)S(1)} %collective-permute-done.1, bf16[1,4,256,1024]{3,2,1,0:T(8,128)(2,1)S(1)} %copy-done.1, bf16[1,4,6,1024]{3,2,1,0:T(8,128)(2,1)S(1)} %collective-permute-done, f32[1024,1024]{1,0:T(8,128)} %fusion.89, f32[4]{0:T(128)S(1)} %get-tuple-element.11, ...), kind=kOutput, calls=%fused_computation.152 | convolution fusion | flops 13549993984 | bytes 35946608 | tf_op jit(solution)/shard_map/tbrc,bcd->tbrd/dot_general | solution.py:43
  45.1 3.8 %fusion.29 = f32[1,4,262,1024]{3,2,1,0:T(8,128)S(1)} fusion(f32[1,4,268,1024]{3,2,1,0:T(8,128)S(1)} %fusion.96, f32[4]{0:T(128)S(1)} %get-tuple-element.42, f32[4]{0:T(128)S(1)} %get-tuple-element.41, f32[4]{0:T(128)S(1)} %get-tuple-element.40, f32[4]{0:T(128)S(1)} %get-tuple-element.39, f32[4]{0:T(128)S(1)} %get-tuple-element.38, ...), kind=kLoop, calls=%fused_computation.66 | loop fusion | flops 15024128 | bytes 34341240 | tf_op jit(solution)/shard_map/jit(_where)/select_n | solution.py:79
  48.9 2.8 %copy.24 = f32[1,4,262,1024]{3,1,2,0:T(4,128)S(1)} copy(f32[1,4,262,1024]{3,2,1,0:T(8,128)S(1)} %fusion.29) | data formatting | bytes 8585216 | tf_op jit(solution)/shard_map/jit(_where)/select_n | solution.py:79
  52.7 2.3 %fusion.100 = f32[4,130,1024]{2,0,1:T(4,128)S(1)} fusion(f32[1,4,131,1024]{3,1,2,0:T(4,128)S(1)} %get-tuple-element.18, f32[1,4,131,1024]{3,1,2,0:T(4,128)S(1)} %get-tuple-element.17), kind=kLoop, calls=%fused_computation.157 | loop fusion | flops 3727360 | bytes 10649600 | tf_op jit(solution)/shard_map/reshape.35
  55.0 5.7 %fusion.119 = f32[4,130,512]{2,1,0:T(8,128)S(1)} fusion(f32[4,130,1024]{2,0,1:T(4,128)S(1)} %fusion.100, s32[512]{0:T(512)S(1)} %iota_multiply_fusion, pred[130]{0:T(512)(128)(4,1)S(1)} %compare_and_fusion), kind=kOutput, calls=%fused_computation.182 | convolution fusion | flops 3278639104 | bytes 3197058 | tf_op jit(solution)/shard_map/dot_general | solution.py:56
  63.5 6.7 %all-to-all-start.2 = ((bf16[1,4,64,256]{3,1,0,2:T(4,128)(2,1)}), bf16[1,4,64,256]{3,1,0,2:T(4,128)(2,1)S(1)}, u32[]{:S(2)}, u32[]{:S(2)}) async-start(bf16[1,4,64,256]{3,1,0,2:T(4,128)(2,1)} %copy.32), calls=%async_computation.2 | async-start | bytes 262144 | tf_op jit(solution)/shard_map/all_to_all | solution.py:133
  71.6 6.8 %all-to-all-done.2 = bf16[1,4,64,256]{3,1,0,2:T(4,128)(2,1)S(1)} async-done(((bf16[1,4,64,256]{3,1,0,2:T(4,128)(2,1)}), bf16[1,4,64,256]{3,1,0,2:T(4,128)(2,1)S(1)}, u32[]{:S(2)}, u32[]{:S(2)}) %all-to-all-start.2) | async-done | bytes 131104 | tf_op jit(solution)/shard_map/all_to_all | solution.py:133
  78.4 3.5 %all-to-all-start.1 = ((bf16[1,4,128,512]{3,1,0,2:T(4,128)(2,1)}), bf16[1,4,128,512]{3,1,0,2:T(4,128)(2,1)S(1)}, u32[]{:S(2)}, u32[]{:S(2)}) async-start(bf16[1,4,128,512]{3,1,0,2:T(4,128)(2,1)} %copy.27), calls=%async_computation.1 | async-start | bytes 1048576 | tf_op jit(solution)/shard_map/all_to_all | solution.py:130
  82.2 2.8 %slice.1298 = bf16[1,4,256,1024]{3,2,1,0:T(8,128)(2,1)S(1)} slice(f32[1,4,262,1024]{3,2,1,0:T(8,128)} %copy-done), slice={[0:1], [0:4], [3:259], [0:1024]} | slice | bytes 4194304 | tf_op jit(solution)/shard_map/slice | solution.py:117
  85.0 2.9 %copy.22 = bf16[1,4,256,1024]{3,1,0,2:T(4,128)(2,1)} copy(bf16[1,4,256,1024]{3,2,1,0:T(8,128)(2,1)S(1)} %slice.1298) | data formatting | bytes 4194304 | tf_op jit(solution)/shard_map/slice | solution.py:117
  88.0 8.6 %all-to-all-done.1 = bf16[1,4,128,512]{3,1,0,2:T(4,128)(2,1)S(1)} async-done(((bf16[1,4,128,512]{3,1,0,2:T(4,128)(2,1)}), bf16[1,4,128,512]{3,1,0,2:T(4,128)(2,1)S(1)}, u32[]{:S(2)}, u32[]{:S(2)}) %all-to-all-start.1) | async-done | bytes 524320 | tf_op jit(solution)/shard_map/all_to_all | solution.py:130
  96.6 4.6 %all-to-all-start = ((bf16[1,4,256,1024]{3,1,0,2:T(4,128)(2,1)}), bf16[1,4,256,1024]{3,1,0,2:T(4,128)(2,1)}, u32[]{:S(2)}, u32[]{:S(2)}) async-start(bf16[1,4,256,1024]{3,1,0,2:T(4,128)(2,1)} %copy.22), calls=%async_computation | async-start | bytes 4194304 | tf_op jit(solution)/shard_map/all_to_all | solution.py:127
  104.2 1.4 add.471
  110.7 2.0 %fusion.129 = bf16[8,4,16,512]{3,2,1,0:T(8,128)(2,1)} fusion(f32[8,4,16,512]{3,2,1,0:T(8,128)S(1)} %fusion.182, f32[4,4,16,512]{3,2,1,0:T(8,128)S(1)} %reshape.284, f32[4,4,16,512]{3,2,1,0:T(8,128)S(1)} %reshape.283), kind=kLoop, calls=%fused_computation.205 | loop fusion | flops 6815744 | bytes 2621440 | tf_op jit(solution)/shard_map/convert_element_type | solution.py:99
  112.7 36.2 %all-to-all-done = bf16[1,4,256,1024]{3,1,0,2:T(4,128)(2,1)} async-done(((bf16[1,4,256,1024]{3,1,0,2:T(4,128)(2,1)}), bf16[1,4,256,1024]{3,1,0,2:T(4,128)(2,1)}, u32[]{:S(2)}, u32[]{:S(2)}) %all-to-all-start) | async-done | bytes 2097184 | tf_op jit(solution)/shard_map/all_to_all | solution.py:127
  149.0 2.8 %convert.18 = f32[1,4,8,32,1024]{4,1,3,2,0:T(4,128)S(1)} convert(bf16[1,4,8,32,1024]{4,1,3,2,0:T(4,128)(2,1)} %bitcast.43) | non-fusion elementwise | flops 1048576 | bytes 6291456 | tf_op jit(solution)/shard_map/convert_element_type | solution.py:83
  151.8 4.5 %bitcast_multiply_fusion = f32[8,4,32,1024]{3,2,1,0:T(8,128)} fusion(f32[1,4,8,32,1024]{4,1,3,2,0:T(4,128)S(1)} %convert.18, f32[8,32,1024]{2,1,0:T(8,128)S(1)} %get-tuple-element.28), kind=kLoop, calls=%fused_computation.121 | loop fusion | flops 1048576 | bytes 9437184 | tf_op jit(solution)/shard_map/mul | solution.py:87
  156.4 13.9 %fusion.75 = f32[8,4,32,1024]{3,2,1,0:T(8,128)S(1)} fusion(f32[8,4,32,1024]{3,2,1,0:T(8,128)} %bitcast_multiply_fusion, f32[1,4,8,32,1024]{4,1,3,2,0:T(4,128)S(1)} %convert.18, f32[8,32,1024]{2,1,0:T(8,128)} %fusion.155, f32[8,32,1024]{2,1,0:T(8,128)} %get-tuple-element.27, f32[8,32,1024]{2,1,0:T(8,128)S(1)} %convert_element_type.202), kind=kLoop, calls=%fused_computation.123 | loop fusion | flops 20971520 | bytes 15728640 | tf_op jit(solution)/shard_map/add | solution.py:94
  170.9 5.8 %fusion.39 = bf16[8,4,32,1024]{3,2,1,0:T(8,128)(2,1)} fusion(f32[8,4,32,1024]{3,2,1,0:T(8,128)S(1)} %fusion.75, f32[4,4,32,1024]{3,2,1,0:T(8,128)S(1)} %reshape.280, f32[4,4,32,1024]{3,2,1,0:T(8,128)S(1)} %reshape.279), kind=kLoop, calls=%fused_computation.82 | loop fusion | flops 27262976 | bytes 10485760 | tf_op jit(solution)/shard_map/convert_element_type | solution.py:99
  (70 shorter events, 16.6 us)
Async XLA Ops:
  1.5 19.6 %collective-permute-start = (bf16[1,4,6,1024]{3,2,1,0:T(8,128)(2,1)S(1)}, bf16[1,4,6,1024]{3,2,1,0:T(8,128)(2,1)S(1)}, u32[]{:S(2)}, u32[]{:S(2)}) collective-permute-start(bf16[1,4,6,1024]{3,2,1,0:T(8,128)(2,1)S(1)} %get-tuple-element.21), channel_id=1, source_target_pairs={{0,1},{2,3},{4,5},{6,7},{8,9},{10,11},{12,13},{14,15},{16,17},{18,... | collective-permute-start | bytes 147464 | tf_op jit(solution)/shard_map/ppermute | solution.py:17
  3.9 17.2 %collective-permute-start.1 = (bf16[1,4,6,1024]{3,2,1,0:T(8,128)(2,1)S(1)}, bf16[1,4,6,1024]{3,2,1,0:T(8,128)(2,1)S(1)}, u32[]{:S(2)}, u32[]{:S(2)}) collective-permute-start(bf16[1,4,6,1024]{3,2,1,0:T(8,128)(2,1)S(1)} %get-tuple-element.22), channel_id=1, source_target_pairs={{1,0},{3,2},{5,4},{7,6},{9,8},{11,10},{13,12},{15,14},{17,16},{19,... | collective-permute-start | bytes 147464 | tf_op jit(solution)/shard_map/ppermute | solution.py:20
  18.2 2.5 %copy-start.5 = (f32[2,4,7]{2,1,0:T(4,128)S(1)}, f32[2,4,7]{2,1,0:T(4,128)}, u32[]{:S(2)}) copy-start(f32[2,4,7]{2,1,0:T(4,128)} %param.4) | copy-start | bytes 676
  18.2 2.9 %copy-start.1 = (bf16[1,4,256,1024]{3,2,1,0:T(8,128)(2,1)S(1)}, bf16[1,4,256,1024]{3,2,1,0:T(8,128)(2,1)}, u32[]{:S(2)}) copy-start(bf16[1,4,256,1024]{3,2,1,0:T(8,128)(2,1)} %param.3) | copy-start | bytes 6291460
  48.9 2.8 %copy-start = (f32[1,4,262,1024]{3,2,1,0:T(8,128)}, f32[1,4,262,1024]{3,2,1,0:T(8,128)S(1)}, u32[]{:S(2)}) copy-start(f32[1,4,262,1024]{3,2,1,0:T(8,128)S(1)} %fusion.29) | copy-start | bytes 12877828
  61.9 20.0 %copy-start.4 = (s32[8,8,8]{2,1,0:T(8,128)S(1)}, s32[8,8,8]{2,1,0:T(8,128)}, u32[]{:S(2)}) copy-start(s32[8,8,8]{2,1,0:T(8,128)} %param.5) | copy-start | bytes 6148
  63.5 14.9 %all-to-all-start.2 = ((bf16[1,4,64,256]{3,1,0,2:T(4,128)(2,1)}), bf16[1,4,64,256]{3,1,0,2:T(4,128)(2,1)S(1)}, u32[]{:S(2)}, u32[]{:S(2)}) async-start(bf16[1,4,64,256]{3,1,0,2:T(4,128)(2,1)} %copy.32), calls=%async_computation.2 | async-start | bytes 262144 | tf_op jit(solution)/shard_map/all_to_all | solution.py:133
  78.4 9.6 %copy-start.2 = (bf16[1,4,64,256]{3,1,0,2:T(4,128)(2,1)}, bf16[1,4,64,256]{3,1,0,2:T(4,128)(2,1)S(1)}, u32[]{:S(2)}) copy-start(bf16[1,4,64,256]{3,1,0,2:T(4,128)(2,1)S(1)} %all-to-all-done.2) | copy-start | bytes 393220
  78.4 18.2 %all-to-all-start.1 = ((bf16[1,4,128,512]{3,1,0,2:T(4,128)(2,1)}), bf16[1,4,128,512]{3,1,0,2:T(4,128)(2,1)S(1)}, u32[]{:S(2)}, u32[]{:S(2)}) async-start(bf16[1,4,128,512]{3,1,0,2:T(4,128)(2,1)} %copy.27), calls=%async_computation.1 | async-start | bytes 1048576 | tf_op jit(solution)/shard_map/all_to_all | solution.py:130
  96.6 52.4 %all-to-all-start = ((bf16[1,4,256,1024]{3,1,0,2:T(4,128)(2,1)}), bf16[1,4,256,1024]{3,1,0,2:T(4,128)(2,1)}, u32[]{:S(2)}, u32[]{:S(2)}) async-start(bf16[1,4,256,1024]{3,1,0,2:T(4,128)(2,1)} %copy.22), calls=%async_computation | async-start | bytes 4194304 | tf_op jit(solution)/shard_map/all_to_all | solution.py:127
  104.2 4.2 %copy-start.3 = (bf16[1,4,64,256]{3,1,0,2:T(4,128)(2,1)S(1)}, bf16[1,4,64,256]{3,1,0,2:T(4,128)(2,1)}, u32[]{:S(2)}) copy-start(bf16[1,4,64,256]{3,1,0,2:T(4,128)(2,1)} %copy-done.2) | copy-start | bytes 393220
where the time goes:
time: 180 us; the launch traced here: 177 us
  other arithmetic  56 us (31%)
  waiting for transfers between devices  51.7 us (29%)
  matrix products  30.5 us (17%)
  local copies, waits for them, and re-layouts  19 us (11%)
  starting transfers between devices  18.4 us (10%)
    all_to_all x1, waiting for transfers between devices, local(): lax.all_to_all(level_zero, 'date', split_axis=2, concat_axis=0, tiled=True)  36.2 us
    dot_general x1, matrix products, column_resample(): jnp.einsum('tbrc,bcd->tbrd', values.astype(jnp.float32), table, precision...  23.9 us
    convert_element_type x4, other arithmetic, column_resample(): (offset == k).astype(jnp.float32)[None]  15.4 us
    add x3, other arithmetic, smooth(): filled = clear4 * values + (1.0 - clear4) * (numer / denom)  14.7 us
    convert_element_type x3, other arithmetic, smooth(): return result.astype(jnp.bfloat16)  8.65 us
    all_to_all x1, waiting for transfers between devices, local(): lax.all_to_all(level_one, 'date', split_axis=2, concat_axis=0, tiled=True)  8.64 us
    all_to_all x1, waiting for transfers between devices, local(): lax.all_to_all(level_two, 'date', split_axis=2, concat_axis=0, tiled=True)  6.81 us
    all_to_all x1, starting transfers between devices, local(): lax.all_to_all(level_two, 'date', split_axis=2, concat_axis=0, tiled=True)  6.67 us
  transfers between devices with their start and end apart: 5, of which 3 were waited for; matrix products, arithmetic and copies ran while one was open for 20% of the time, Pallas kernels for 0%

commit v1 on v0

--- a/solution.py
+++ b/solution.py
@@ -7,6 +7,22 @@
 gap_weights = [math.exp(-((k - 4) ** 2) / 8.0) for k in range(9)]
 savgol_coeffs = [c / 231.0 for c in [-21.0, 14.0, 39.0, 54.0, 59.0, 54.0, 39.0, 14.0, -21.0]]
 pyramid_filter = [0.125, 0.375, 0.375, 0.125]
+
+
+def pairwise_exchange(array, axis, split, join):
+    ways, here = (lax.axis_size(axis), lax.axis_index(axis))
+    width = array.shape[split] // ways
+    dims = list(array.shape)
+    dims[split] = width
+    height = dims[join]
+    dims[join] = height * ways
+    full = jnp.zeros(dims, array.dtype)
+    for mask in range(ways):
+        part = lax.dynamic_slice_in_dim(array, (here ^ mask) * width, width, axis=split)
+        if mask:
+            part = lax.ppermute(part, axis, [(d, d ^ mask) for d in range(ways)])
+        full = lax.dynamic_update_slice_in_dim(full, part, (here ^ mask) * height, axis=join)
+    return full
 
 
 def padded(block, sides, width):
@@ -123,9 +139,7 @@
     clear_fine = expand_mask(clear_mask, 4, 128)
     clear_half = expand_mask(clear_mask, 2, 64)
     clear_quarter = expand_mask(clear_mask, 1, 32)
-    smooth_fine = smooth(
-        lax.all_to_all(level_zero, "date", split_axis=2, concat_axis=0, tiled=True), clear_fine
-    )
+    smooth_fine = smooth(pairwise_exchange(level_zero, "date", 2, 0), clear_fine)
     smooth_half = smooth(
         lax.all_to_all(level_one, "date", split_axis=2, concat_axis=0, tiled=True), clear_half
     )

time: 180 us -> 168 us (0.933)
  the two profiles are of different devices: /device:TPU:0 before, /device:TPU:16 now
where the time goes in v1:
time: 168 us; the launch traced here: 167 us
  other arithmetic  47.3 us (28%)
  waiting for transfers between devices  43.4 us (26%)
  matrix products  30.9 us (18%)
  starting transfers between devices  23.2 us (14%)
  local copies, waits for them, and re-layouts  20.9 us (12%)
    ppermute x7, waiting for transfers between devices, pairwise_exchange(): part = lax.ppermute(part, axis, [(d, d ^ mask) for d in range(ways)])  43.4 us
    dot_general x1, matrix products, column_resample(): jnp.einsum('tbrc,bcd->tbrd', values.astype(jnp.float32), table, precision...  24.4 us
    convert_element_type x4, other arithmetic, column_resample(): (offset == k).astype(jnp.float32)[None]  15.4 us
    convert_element_type x3, other arithmetic, smooth(): return result.astype(jnp.bfloat16)  8.52 us
    ppermute x7, starting transfers between devices, pairwise_exchange(): part = lax.ppermute(part, axis, [(d, d ^ mask) for d in range(ways)])  8.35 us
    add x3, other arithmetic, smooth(): filled = clear4 * values + (1.0 - clear4) * (numer / denom)  6.97 us
    dot_general x2, matrix products, halve_columns(): return jnp.dot(values, table, precision=lax.Precision.HIGHEST)  6.56 us
    all_to_all x1, starting transfers between devices, local(): lax.all_to_all(level_two, 'date', split_axis=2, concat_axis=0, tiled=True)  6.17 us
  transfers between devices with their start and end apart: 11, of which 5 were waited for; matrix products, arithmetic and copies ran while one was open for 30% of the time, Pallas kernels for 0%

profile of v1, /device:TPU:16, one launch (start us, length us, event | category | flops | bytes accessed | tf_op | source)
XLA Modules:
  0.0 167.0 jit_solution(6161278882215309778)
XLA Ops:
  0.6 1.5 fusion.313
  2.2 2.4 %collective-permute-start = (bf16[1,4,6,1024]{3,2,1,0:T(8,128)(2,1)}, bf16[1,4,6,1024]{3,2,1,0:T(8,128)(2,1)}, u32[]{:S(2)}, u32[]{:S(2)}) collective-permute-start(bf16[1,4,6,1024]{3,2,1,0:T(8,128)(2,1)} %get-tuple-element.29), channel_id=1, source_target_pairs={{0,1},{2,3},{4,5},{6,7},{8,9},{10,11},{12,13},{14,15},{16,17},{18,... | collective-permute-start | bytes 147464 | tf_op jit(solution)/shard_map/ppermute | solution.py:33
  5.8 4.3 %fusion.83 = (f32[1024,1024]{1,0:T(8,128)}, f32[1024,1024]{1,0:T(8,128)}) fusion(), kind=kLoop, calls=%fused_computation.132 | loop fusion | flops 6291456 | bytes 8388608 | tf_op jit(solution)/shard_map/convert_element_type | solution.py:58
  10.2 4.3 %fusion.85 = (f32[1024,1024]{1,0:T(8,128)}, f32[1024,1024]{1,0:T(8,128)}) fusion(), kind=kLoop, calls=%fused_computation.134 | loop fusion | flops 6291456 | bytes 8388608 | tf_op jit(solution)/shard_map/convert_element_type | solution.py:58
  14.4 4.3 %fusion.87 = (f32[1024,1024]{1,0:T(8,128)}, f32[1024,1024]{1,0:T(8,128)}) fusion(), kind=kLoop, calls=%fused_computation.136 | loop fusion | flops 6291456 | bytes 8388608 | tf_op jit(solution)/shard_map/convert_element_type | solution.py:58
  18.8 2.5 %fusion.89 = f32[1024,1024]{1,0:T(8,128)} fusion(), kind=kLoop, calls=%fused_computation.138 | loop fusion | flops 4194304 | bytes 4194304 | tf_op jit(solution)/shard_map/convert_element_type | solution.py:58
  26.7 1.7 %broadcast_subtract_fusion = (f32[8,32,1024]{2,1,0:T(8,128)}, f32[8,32,1024]{2,1,0:T(8,128)}) fusion(f32[8,32,1024]{2,1,0:T(8,128)S(1)} %convert_element_type.193), kind=kLoop, calls=%fused_computation.305 | loop fusion | flops 786432 | bytes 3145728 | tf_op jit(solution)/shard_map/sub | solution.py:110
  30.7 24.4 %fusion.96 = f32[1,4,268,1024]{3,2,1,0:T(8,128)S(1)} fusion(bf16[1,4,6,1024]{3,2,1,0:T(8,128)(2,1)} %collective-permute-done.1, bf16[1,4,256,1024]{3,2,1,0:T(8,128)(2,1)} %param.3, bf16[1,4,6,1024]{3,2,1,0:T(8,128)(2,1)} %collective-permute-done, f32[1024,1024]{1,0:T(8,128)} %fusion.89, f32[4]{0:T(128)S(1)} %get-tuple-element.11, ...), kind=kOutput, calls=%fused_computation.152 | convolution fusion | flops 13549993984 | bytes 35946608 | tf_op jit(solution)/shard_map/tbrc,bcd->tbrd/dot_general | solution.py:59
  55.1 3.8 %fusion.29 = f32[1,4,262,1024]{3,2,1,0:T(8,128)S(1)} fusion(f32[1,4,268,1024]{3,2,1,0:T(8,128)S(1)} %fusion.96, f32[4]{0:T(128)S(1)} %get-tuple-element.50, f32[4]{0:T(128)S(1)} %get-tuple-element.49, f32[4]{0:T(128)S(1)} %get-tuple-element.48, f32[4]{0:T(128)S(1)} %get-tuple-element.47, f32[4]{0:T(128)S(1)} %get-tuple-element.46, ...), kind=kLoop, calls=%fused_computation.68 | loop fusion | flops 15024128 | bytes 34341240 | tf_op jit(solution)/shard_map/jit(_where)/select_n | solution.py:95
  58.9 2.8 %copy.20 = f32[1,4,262,1024]{3,1,2,0:T(4,128)S(1)} copy(f32[1,4,262,1024]{3,2,1,0:T(8,128)S(1)} %fusion.29) | data formatting | bytes 8585216 | tf_op jit(solution)/shard_map/jit(_where)/select_n | solution.py:95
  62.7 2.3 %fusion.100 = f32[4,130,1024]{2,0,1:T(4,128)S(1)} fusion(f32[1,4,131,1024]{3,1,2,0:T(4,128)S(1)} %get-tuple-element.18, f32[1,4,131,1024]{3,1,2,0:T(4,128)S(1)} %get-tuple-element.17), kind=kLoop, calls=%fused_computation.157 | loop fusion | flops 3727360 | bytes 10649600 | tf_op jit(solution)/shard_map/reshape.35
  65.1 5.7 %fusion.119 = f32[4,130,512]{2,1,0:T(8,128)S(1)} fusion(f32[4,130,1024]{2,0,1:T(4,128)S(1)} %fusion.100, s32[512]{0:T(512)S(1)} %iota_multiply_fusion, pred[130]{0:T(512)(128)(4,1)S(1)} %compare_and_fusion), kind=kOutput, calls=%fused_computation.182 | convolution fusion | flops 3278639104 | bytes 3197058 | tf_op jit(solution)/shard_map/dot_general | solution.py:72
  73.6 6.2 %all-to-all-start.1 = ((bf16[1,4,64,256]{3,1,0,2:T(4,128)(2,1)}), bf16[1,4,64,256]{3,1,0,2:T(4,128)(2,1)}, u32[]{:S(2)}, u32[]{:S(2)}) async-start(bf16[1,4,64,256]{3,1,0,2:T(4,128)(2,1)} %copy.28), calls=%async_computation.1 | async-start | bytes 262144 | tf_op jit(solution)/shard_map/all_to_all | solution.py:147
  79.8 2.8 %slice.1298 = bf16[1,4,256,1024]{3,2,1,0:T(8,128)(2,1)S(1)} slice(f32[1,4,262,1024]{3,2,1,0:T(8,128)} %copy-done), slice={[0:1], [0:4], [3:259], [0:1024]} | slice | bytes 4194304 | tf_op jit(solution)/shard_map/slice | solution.py:133
  89.0 3.8 %collective-permute-start.6 = (bf16[1,4,32,1024]{3,2,1,0:T(8,128)(2,1)}, bf16[1,4,32,1024]{3,2,1,0:T(8,128)(2,1)}, u32[]{:S(2)}, u32[]{:S(2)}) collective-permute-start(bf16[1,4,32,1024]{3,2,1,0:T(8,128)(2,1)} %get-tuple-element.23), channel_id=1, source_target_pairs={{0,10},{2,8},{4,14},{6,12},{8,2},{10,0},{12,6},{14,4},{1,11},{3,9}... | collective-permute-start | bytes 786440 | tf_op jit(solution)/shard_map/ppermute | solution.py:23
  92.9 5.1 %all-to-all-start = ((bf16[1,4,128,512]{3,1,0,2:T(4,128)(2,1)}), bf16[1,4,128,512]{3,1,0,2:T(4,128)(2,1)}, u32[]{:S(2)}, u32[]{:S(2)}) async-start(bf16[1,4,128,512]{3,1,0,2:T(4,128)(2,1)} %copy.23), calls=%async_computation | async-start | bytes 1048576 | tf_op jit(solution)/shard_map/all_to_all | solution.py:144
  102.4 2.0 %collective-permute-done.3 = bf16[1,4,32,1024]{3,2,1,0:T(8,128)(2,1)} collective-permute-done((bf16[1,4,32,1024]{3,2,1,0:T(8,128)(2,1)}, bf16[1,4,32,1024]{3,2,1,0:T(8,128)(2,1)}, u32[]{:S(2)}, u32[]{:S(2)}) %collective-permute-start.3) | collective-permute-done | bytes 262176 | tf_op jit(solution)/shard_map/ppermute | solution.py:23
  105.8 4.2 %collective-permute-done.4 = bf16[1,4,32,1024]{3,2,1,0:T(8,128)(2,1)} collective-permute-done((bf16[1,4,32,1024]{3,2,1,0:T(8,128)(2,1)}, bf16[1,4,32,1024]{3,2,1,0:T(8,128)(2,1)}, u32[]{:S(2)}, u32[]{:S(2)}) %collective-permute-start.4) | collective-permute-done | bytes 262176 | tf_op jit(solution)/shard_map/ppermute | solution.py:23
  112.0 1.5 collective-permute-done.6
  114.5 29.9 %collective-permute-done.7 = bf16[1,4,32,1024]{3,2,1,0:T(8,128)(2,1)S(1)} collective-permute-done((bf16[1,4,32,1024]{3,2,1,0:T(8,128)(2,1)}, bf16[1,4,32,1024]{3,2,1,0:T(8,128)(2,1)S(1)}, u32[]{:S(2)}, u32[]{:S(2)}) %collective-permute-start.7) | collective-permute-done | bytes 262176 | tf_op jit(solution)/shard_map/ppermute | solution.py:23
  144.4 5.8 %collective-permute-done.8 = bf16[1,4,32,1024]{3,2,1,0:T(8,128)(2,1)S(1)} collective-permute-done((bf16[1,4,32,1024]{3,2,1,0:T(8,128)(2,1)}, bf16[1,4,32,1024]{3,2,1,0:T(8,128)(2,1)S(1)}, u32[]{:S(2)}, u32[]{:S(2)}) %collective-permute-start.8) | collective-permute-done | bytes 262176 | tf_op jit(solution)/shard_map/ppermute | solution.py:23
  150.9 5.3 %fusion.35 = f32[8,4,32,1024]{3,2,1,0:T(8,128)S(1)} fusion(bf16[8,4,32,1024]{3,2,1,0:T(8,128)(2,1)S(1)} %constant_dynamic-update-slice_fusion, f32[8,4,32,1024]{3,2,1,0:T(8,128)S(1)} %convert_multiply_fusion, f32[8,32,1024]{2,1,0:T(8,128)} %fusion.155, f32[8,32,1024]{2,1,0:T(8,128)} %get-tuple-element.35, f32[8,32,1024]{2,1,0:T(8,128)S(1)} %convert_element_type.193), kind=kLoop, calls=%fused_computation.80 | loop fusion | flops 22020096 | bytes 13631488 | tf_op jit(solution)/shard_map/add | solution.py:110
  156.9 5.7 %fusion.40 = bf16[8,4,32,1024]{3,2,1,0:T(8,128)(2,1)} fusion(f32[8,4,32,1024]{3,2,1,0:T(8,128)S(1)} %fusion.35, f32[4,4,32,1024]{3,2,1,0:T(8,128)S(1)} %reshape.276, f32[4,4,32,1024]{3,2,1,0:T(8,128)S(1)} %reshape.275), kind=kLoop, calls=%fused_computation.85 | loop fusion | flops 27262976 | bytes 10485760 | tf_op jit(solution)/shard_map/convert_element_type | solution.py:115
  165.0 2.0 %fusion.129 = bf16[8,4,16,512]{3,2,1,0:T(8,128)(2,1)} fusion(f32[8,4,16,512]{3,2,1,0:T(8,128)S(1)} %fusion.182, f32[4,4,16,512]{3,2,1,0:T(8,128)S(1)} %reshape.280, f32[4,4,16,512]{3,2,1,0:T(8,128)S(1)} %reshape.279), kind=kLoop, calls=%fused_computation.205 | loop fusion | flops 6815744 | bytes 2621440 | tf_op jit(solution)/shard_map/convert_element_type | solution.py:115
  (93 shorter events, 31.5 us)
Async XLA Ops:
  2.2 28.5 %collective-permute-start = (bf16[1,4,6,1024]{3,2,1,0:T(8,128)(2,1)}, bf16[1,4,6,1024]{3,2,1,0:T(8,128)(2,1)}, u32[]{:S(2)}, u32[]{:S(2)}) collective-permute-start(bf16[1,4,6,1024]{3,2,1,0:T(8,128)(2,1)} %get-tuple-element.29), channel_id=1, source_target_pairs={{0,1},{2,3},{4,5},{6,7},{8,9},{10,11},{12,13},{14,15},{16,17},{18,... | collective-permute-start | bytes 147464 | tf_op jit(solution)/shard_map/ppermute | solution.py:33
  4.5 26.2 %collective-permute-start.1 = (bf16[1,4,6,1024]{3,2,1,0:T(8,128)(2,1)}, bf16[1,4,6,1024]{3,2,1,0:T(8,128)(2,1)}, u32[]{:S(2)}, u32[]{:S(2)}) collective-permute-start(bf16[1,4,6,1024]{3,2,1,0:T(8,128)(2,1)} %get-tuple-element.30), channel_id=1, source_target_pairs={{1,0},{3,2},{5,4},{7,6},{9,8},{11,10},{13,12},{15,14},{17,16},{19,... | collective-permute-start | bytes 147464 | tf_op jit(solution)/shard_map/ppermute | solution.py:36
  18.8 3.0 %copy-start.5 = (s32[8,8,8]{2,1,0:T(8,128)S(1)}, s32[8,8,8]{2,1,0:T(8,128)}, u32[]{:S(2)}) copy-start(s32[8,8,8]{2,1,0:T(8,128)} %param.5) | copy-start | bytes 6148
  18.8 3.1 %copy-start.6 = (f32[2,4,7]{2,1,0:T(4,128)S(1)}, f32[2,4,7]{2,1,0:T(4,128)}, u32[]{:S(2)}) copy-start(f32[2,4,7]{2,1,0:T(4,128)} %param.4) | copy-start | bytes 676
  58.9 2.8 %copy-start = (f32[1,4,262,1024]{3,2,1,0:T(8,128)}, f32[1,4,262,1024]{3,2,1,0:T(8,128)S(1)}, u32[]{:S(2)}) copy-start(f32[1,4,262,1024]{3,2,1,0:T(8,128)S(1)} %fusion.29) | copy-start | bytes 12877828
  70.7 1.2 copy-start.7
  73.6 19.3 %all-to-all-start.1 = ((bf16[1,4,64,256]{3,1,0,2:T(4,128)(2,1)}), bf16[1,4,64,256]{3,1,0,2:T(4,128)(2,1)}, u32[]{:S(2)}, u32[]{:S(2)}) async-start(bf16[1,4,64,256]{3,1,0,2:T(4,128)(2,1)} %copy.28), calls=%async_computation.1 | async-start | bytes 262144 | tf_op jit(solution)/shard_map/all_to_all | solution.py:147
  85.5 15.4 %collective-permute-start.2 = (bf16[1,4,32,1024]{3,2,1,0:T(8,128)(2,1)}, bf16[1,4,32,1024]{3,2,1,0:T(8,128)(2,1)}, u32[]{:S(2)}, u32[]{:S(2)}) collective-permute-start(bf16[1,4,32,1024]{3,2,1,0:T(8,128)(2,1)} %get-tuple-element.27), channel_id=1, source_target_pairs={{0,2},{2,0},{4,6},{6,4},{8,10},{10,8},{12,14},{14,12},{1,3},{3,1},... | collective-permute-start | bytes 786440 | tf_op jit(solution)/shard_map/ppermute | solution.py:23
  87.0 17.4 %collective-permute-start.3 = (bf16[1,4,32,1024]{3,2,1,0:T(8,128)(2,1)}, bf16[1,4,32,1024]{3,2,1,0:T(8,128)(2,1)}, u32[]{:S(2)}, u32[]{:S(2)}) collective-permute-start(bf16[1,4,32,1024]{3,2,1,0:T(8,128)(2,1)} %get-tuple-element.26), channel_id=1, source_target_pairs={{0,4},{2,6},{4,0},{6,2},{8,12},{10,14},{12,8},{14,10},{1,5},{3,7},... | collective-permute-start | bytes 786440 | tf_op jit(solution)/shard_map/ppermute | solution.py:23
  88.5 21.5 %collective-permute-start.4 = (bf16[1,4,32,1024]{3,2,1,0:T(8,128)(2,1)}, bf16[1,4,32,1024]{3,2,1,0:T(8,128)(2,1)}, u32[]{:S(2)}, u32[]{:S(2)}) collective-permute-start(bf16[1,4,32,1024]{3,2,1,0:T(8,128)(2,1)} %get-tuple-element.25), channel_id=1, source_target_pairs={{0,6},{2,4},{4,2},{6,0},{8,14},{10,12},{12,10},{14,8},{1,7},{3,5},... | collective-permute-start | bytes 786440 | tf_op jit(solution)/shard_map/ppermute | solution.py:23
  89.0 22.0 %collective-permute-start.5 = (bf16[1,4,32,1024]{3,2,1,0:T(8,128)(2,1)}, bf16[1,4,32,1024]{3,2,1,0:T(8,128)(2,1)}, u32[]{:S(2)}, u32[]{:S(2)}) collective-permute-start(bf16[1,4,32,1024]{3,2,1,0:T(8,128)(2,1)} %get-tuple-element.24), channel_id=1, source_target_pairs={{0,8},{2,10},{4,12},{6,14},{8,0},{10,2},{12,4},{14,6},{1,9},{3,11}... | collective-permute-start | bytes 786440 | tf_op jit(solution)/shard_map/ppermute | solution.py:23
  89.0 24.5 %collective-permute-start.6 = (bf16[1,4,32,1024]{3,2,1,0:T(8,128)(2,1)}, bf16[1,4,32,1024]{3,2,1,0:T(8,128)(2,1)}, u32[]{:S(2)}, u32[]{:S(2)}) collective-permute-start(bf16[1,4,32,1024]{3,2,1,0:T(8,128)(2,1)} %get-tuple-element.23), channel_id=1, source_target_pairs={{0,10},{2,8},{4,14},{6,12},{8,2},{10,0},{12,6},{14,4},{1,11},{3,9}... | collective-permute-start | bytes 786440 | tf_op jit(solution)/shard_map/ppermute | solution.py:23
  92.9 69.8 %all-to-all-start = ((bf16[1,4,128,512]{3,1,0,2:T(4,128)(2,1)}), bf16[1,4,128,512]{3,1,0,2:T(4,128)(2,1)}, u32[]{:S(2)}, u32[]{:S(2)}) async-start(bf16[1,4,128,512]{3,1,0,2:T(4,128)(2,1)} %copy.23), calls=%async_computation | async-start | bytes 1048576 | tf_op jit(solution)/shard_map/all_to_all | solution.py:144
  98.0 52.3 %copy-start.1 = (f32[8,32,1024]{2,1,0:T(8,128)S(1)}, f32[8,32,1024]{2,1,0:T(8,128)}, u32[]{:S(2)}) copy-start(f32[8,32,1024]{2,1,0:T(8,128)} %get-tuple-element.36) | copy-start | bytes 3145732
  100.9 43.4 %collective-permute-start.7 = (bf16[1,4,32,1024]{3,2,1,0:T(8,128)(2,1)}, bf16[1,4,32,1024]{3,2,1,0:T(8,128)(2,1)S(1)}, u32[]{:S(2)}, u32[]{:S(2)}) collective-permute-start(bf16[1,4,32,1024]{3,2,1,0:T(8,128)(2,1)} %get-tuple-element.22), channel_id=1, source_target_pairs={{0,12},{2,14},{4,8},{6,10},{8,4},{10,6},{12,0},{14,2},{1,13},{3,15... | collective-permute-start | bytes 786440 | tf_op jit(solution)/shard_map/ppermute | solution.py:23
  104.4 45.8 %collective-permute-start.8 = (bf16[1,4,32,1024]{3,2,1,0:T(8,128)(2,1)}, bf16[1,4,32,1024]{3,2,1,0:T(8,128)(2,1)S(1)}, u32[]{:S(2)}, u32[]{:S(2)}) collective-permute-start(bf16[1,4,32,1024]{3,2,1,0:T(8,128)(2,1)} %get-tuple-element.21), channel_id=1, source_target_pairs={{0,14},{2,12},{4,10},{6,8},{8,6},{10,4},{12,2},{14,0},{1,15},{3,13... | collective-permute-start | bytes 786440 | tf_op jit(solution)/shard_map/ppermute | solution.py:23
  156.9 6.9 %copy-start.2 = (f32[8,16,512]{2,1,0:T(8,128)S(1)}, f32[8,16,512]{2,1,0:T(8,128)}, u32[]{:S(2)}) copy-start(f32[8,16,512]{2,1,0:T(8,128)} %get-tuple-element.40) | copy-start | bytes 786436
  156.9 7.3 %copy-start.3 = (f32[8,16,512]{2,1,0:T(8,128)S(1)}, f32[8,16,512]{2,1,0:T(8,128)}, u32[]{:S(2)}) copy-start(f32[8,16,512]{2,1,0:T(8,128)} %get-tuple-element.39) | copy-start | bytes 786436
  156.9 7.3 %copy-start.4 = (f32[8,16,512]{2,1,0:T(8,128)S(1)}, f32[8,16,512]{2,1,0:T(8,128)}, u32[]{:S(2)}) copy-start(f32[8,16,512]{2,1,0:T(8,128)} %fusion.242) | copy-start | bytes 786436
